TPU v7x, 128 devices: a whole 4x4x4 slice. The times are simulated.
128 devices in a mesh: seq: 16 (over x, y), exp: 8 (over z, core).
Axes of the slice: x: 4, y: 4, z: 4, core: 2. Of those that a mesh axis runs over, the one named last changes fastest.
Arguments:
- hidden: bfloat16 [2048, 4096], P('seq', 'exp'), may hold values from -6 to 6
- queries: bfloat16 [2048, 4096], P('seq', 'exp'), may hold values from -40 to 40
- keys: bfloat16 [2048, 1024], P('seq', 'exp'), may hold values from -6 to 6
- values: bfloat16 [2048, 1024], P('seq', 'exp'), may hold values from -6 to 6
- block_place: int32 [32], replicated, may hold values from 0 to 31, as said below
- page_table: int32 [128], replicated, may hold values from 0 to 127, each once
- out_weight: bfloat16 [4096, 4096], P('exp'), may hold values from -0.09375 to 0.09375
- norm_gain: float32 [4096], replicated, may hold values from 0.5 to 2
- gate_probs: float32 [2048, 2], P('seq'), may hold values from 0.1 to 1
- routes: int32 [2048, 2], P('seq'), may hold values from 0 to 7, all different within a row; in each aligned block of 128 rows (0 to 127, 128 to 255, ...) at most 64 rows name the same one
- w_gate: bfloat16 [8, 4096, 14336], P('exp', None, 'seq'), may hold values from -0.09375 to 0.09375
- w_up: bfloat16 [8, 4096, 14336], P('exp', None, 'seq'), may hold values from -0.09375 to 0.09375
- w_down: bfloat16 [8, 14336, 4096], P('exp', 'seq'), may hold values from -0.046875 to 0.046875
Outputs:
- layer_out: bfloat16 [2048, 4096], P('seq', 'exp')
- key_value_pages: bfloat16 [128, 16, 2, 1024], P('seq', None, None, 'exp')
Inputs may be any that keep to these rules, and one draw needn't show every extreme that they name: `block_place`: the first 24 entries are a permutation of 0 to 23, the others a permutation of 24 to 31. `page_table`: A permutation of the pages. `routes`: in the rows of one index of seq (128 rows) no expert is named more than 64 times, a bound that some block reaches; a row names two different experts.
All inputs are finite; a program needn't handle non-finite values.
Results may differ from a plain program's by a relative error of at most 0.02.
Values may be sent and summed in bfloat16 or wider, within the bound.
No kernel may reach another device: no remote copies, remote signals or barrier semaphores. Data moves between devices by JAX's collectives and lax.ppermute only.
A program may use at most 128 MiB of HBM per device.

v0:
```python
import math
import jax
import jax.numpy as jnp
from jax import lax
from jax.sharding import PartitionSpec as P

HEAD_SIZE = 128
NEXP = 8
PAGE_TOKENS = 16
THETA = 1000000.0
EPS = 1e-05


def apply_rotary(values_in, positions, head_count):
    row_count = values_in.shape[0]
    split_view = values_in.astype(jnp.float32).reshape(row_count, head_count, HEAD_SIZE)
    steps_half = jnp.arange(HEAD_SIZE // 2, dtype=jnp.float32)
    frequency = THETA ** (-(2.0 * steps_half) / HEAD_SIZE)
    angles = positions.astype(jnp.float32)[:, None] * frequency[None, :]
    cosine = jnp.cos(angles)[:, None, :]
    sine_part = jnp.sin(angles)[:, None, :]
    front_half = split_view[..., : HEAD_SIZE // 2]
    back_half = split_view[..., HEAD_SIZE // 2 :]
    turned = jnp.concatenate(
        [front_half * cosine - back_half * sine_part, back_half * cosine + front_half * sine_part],
        axis=-1,
    )
    return turned.reshape(row_count, head_count * HEAD_SIZE).astype(jnp.bfloat16)


def per_device(
    hidden,
    queries,
    keys,
    values,
    block_place,
    page_table,
    out_weight,
    norm_gain,
    gate_probs,
    routes,
    w_gate,
    w_up,
    w_down,
):
    seq_count = lax.axis_size("seq")
    exp_count = lax.axis_size("exp")
    seq_index = lax.axis_index("seq")
    tok_rows = queries.shape[0]
    half_rows = tok_rows // 2
    all_rows = tok_rows * seq_count
    long_len = 3 * all_rows // 4
    every_row = jnp.arange(all_rows, dtype=jnp.int32)
    all_pos = block_place[every_row // half_rows] * half_rows + every_row % half_rows
    my_pos = lax.dynamic_slice_in_dim(all_pos, seq_index * tok_rows, tok_rows)
    my_long = my_pos >= long_len
    my_rope = my_pos - long_len * my_long.astype(jnp.int32)
    q_heads = queries.shape[1] // HEAD_SIZE
    kv_heads = keys.shape[1] // HEAD_SIZE
    query_head_group = q_heads // kv_heads
    query_rotated = apply_rotary(queries, my_rope, q_heads)
    key_rotated = apply_rotary(keys, my_rope, kv_heads)
    q_grid = query_rotated.reshape(tok_rows, kv_heads, query_head_group, HEAD_SIZE)
    score_scale = 1.0 / math.sqrt(HEAD_SIZE)
    page_count = tok_rows // PAGE_TOKENS
    inverse_table = jnp.argsort(page_table)
    my_logical = lax.dynamic_slice_in_dim(inverse_table, seq_index * page_count, page_count)
    row_at = jnp.argsort(all_pos)
    taken = row_at[
        (
            my_logical[:, None] * PAGE_TOKENS + jnp.arange(PAGE_TOKENS, dtype=jnp.int32)[None, :]
        ).reshape(page_count * PAGE_TOKENS)
    ]
    key_all, value_all = (
        lax.all_gather(key_rotated, "seq", axis=0, tiled=True),
        lax.all_gather(values, "seq", axis=0, tiled=True),
    )
    peak_old = jnp.full((kv_heads, query_head_group, tok_rows), -1e30, jnp.float32)
    row_count = key_all.shape[0]
    scores = (
        jnp.einsum(
            "tkgd,nkd->kgtn",
            q_grid,
            key_all.reshape(row_count, kv_heads, HEAD_SIZE),
            preferred_element_type=jnp.float32,
        )
        * score_scale
    )
    allowed = ((all_pos >= long_len)[None, :] == my_long[:, None]) & (
        all_pos[None, :] <= my_pos[:, None]
    )
    scores = jnp.where(allowed, scores, -1e30)
    peak_new = jnp.maximum(peak_old, jnp.max(scores, axis=-1))
    weights = jnp.where(allowed, jnp.exp(scores - peak_new[..., None]), 0.0)
    total_new = jnp.sum(weights, axis=-1)
    summed = jnp.einsum(
        "kgtn,nkd->kgtd",
        weights.astype(jnp.bfloat16),
        value_all.reshape(row_count, kv_heads, HEAD_SIZE),
        preferred_element_type=jnp.float32,
    )
    peak_final, total_final, summed = (peak_new, total_new, summed)
    cache_pages = jnp.stack([key_all[taken], value_all[taken]], axis=1).reshape(
        page_count, PAGE_TOKENS, 2, kv_heads * HEAD_SIZE
    )
    attended = (
        (summed / total_final[..., None])
        .transpose(2, 0, 1, 3)
        .reshape(tok_rows, q_heads * HEAD_SIZE)
        .astype(jnp.bfloat16)
    )
    partial_proj = jnp.dot(attended, out_weight, preferred_element_type=jnp.float32)
    projected = lax.psum_scatter(
        partial_proj.astype(jnp.bfloat16), "exp", scatter_dimension=1, tiled=True
    ).astype(jnp.float32)
    residual = (hidden.astype(jnp.float32) + projected).astype(jnp.bfloat16)
    top_count = routes.shape[1]
    capacity = tok_rows // 2
    assign_count = tok_rows * top_count
    flat_routes = routes.reshape(assign_count)
    expert_hot = (flat_routes[:, None] == jnp.arange(NEXP, dtype=jnp.int32)[None, :]).astype(
        jnp.float32
    )
    earlier = (jnp.arange(assign_count)[:, None] > jnp.arange(assign_count)[None, :]).astype(
        jnp.float32
    )
    before = jnp.dot(earlier, expert_hot, preferred_element_type=jnp.float32)
    slot_rank = jnp.sum(before * expert_hot, axis=1).astype(jnp.int32).reshape(tok_rows, top_count)
    slot_grid = routes * capacity + slot_rank
    chooser = jnp.any(
        slot_grid[None, :, :] == jnp.arange(NEXP * capacity, dtype=jnp.int32)[:, None, None],
        axis=-1,
    ).astype(jnp.bfloat16)
    outgoing_rows = jnp.dot(chooser, residual, preferred_element_type=jnp.float32).astype(
        jnp.bfloat16
    )
    expert_local = NEXP // exp_count
    arrived_rows = lax.all_to_all(
        outgoing_rows.reshape(exp_count, expert_local * capacity, -1),
        "exp",
        split_axis=0,
        concat_axis=2,
        tiled=True,
    )
    gathered_in = arrived_rows.astype(jnp.float32)
    mean_square = jnp.mean(gathered_in * gathered_in, axis=-1, keepdims=True)
    normed = (gathered_in * lax.rsqrt(mean_square + EPS) * norm_gain).astype(jnp.bfloat16)
    token_rows = lax.all_gather(normed, "seq", axis=1, tiled=True)
    gate_part = jnp.einsum("end,edf->enf", token_rows, w_gate, preferred_element_type=jnp.float32)
    up_part = jnp.einsum("end,edf->enf", token_rows, w_up, preferred_element_type=jnp.float32)
    hidden_units = (jax.nn.silu(gate_part) * up_part).astype(jnp.bfloat16)
    returned = lax.psum_scatter(
        jnp.einsum("enf,efd->ned", hidden_units, w_down, preferred_element_type=jnp.float32).astype(
            jnp.bfloat16
        ),
        "seq",
        scatter_dimension=0,
        tiled=True,
    )
    homed = lax.all_to_all(returned, "exp", split_axis=2, concat_axis=1, tiled=True)
    lookup = homed.reshape(capacity * NEXP, -1)
    chosen = (
        lookup[(slot_rank * NEXP + routes).reshape(assign_count)]
        .astype(jnp.float32)
        .reshape(tok_rows, top_count, -1)
    )
    gate_share = gate_probs / jnp.sum(gate_probs, axis=1, keepdims=True)
    layer_out = (
        residual.astype(jnp.float32) + jnp.sum(gate_share[:, :, None] * chosen, axis=1)
    ).astype(jnp.bfloat16)
    return (layer_out, cache_pages)


def solution(mesh):
    return jax.shard_map(
        per_device,
        mesh=mesh,
        in_specs=(
            P("seq", "exp"),
            P("seq", "exp"),
            P("seq", "exp"),
            P("seq", "exp"),
            P(),
            P(),
            P("exp", None),
            P(),
            P("seq", None),
            P("seq", None),
            P("exp", None, "seq"),
            P("exp", None, "seq"),
            P("exp", "seq", None),
        ),
        out_specs=(P("seq", "exp"), P("seq", None, None, "exp")),
        check_vma=False,
    )
```

profile of v0, /device:TPU:1, one launch (start us, length us, event | category | flops | bytes accessed | tf_op | source)
XLA Modules:
  0.0 390.9 jit_solution(8095771630104824144)
XLA Ops:
  8.4 1.8 fusion.55
  10.2 2.1 fusion.54
  12.3 4.3 %compare_select_fusion.1 = s32[2048,1]{0,1:T(1,128)S(1)} fusion(s32[]{:T(128)} %bitcast.25, s32[]{:T(128)} %bitcast.26, s32[]{:T(128)} %bitcast.27, s32[]{:T(128)} %bitcast.28, s32[]{:T(128)} %bitcast.29, s32[]{:T(128)} %bitcast.31, s32[]{:T(128)} %bitcast.30), kind=kLoop, calls=%fused_computation.88 | loop fusion | flops 47104 | bytes 8220 | tf_op jit(solution)/shard_map/gather | solution.py:54
  16.7 15.8 %broadcast_compare_fusion = (pred[2048]{0:T(1024)(128)(4,1)S(1)}, s32[2048]{0:T(1024)S(1)}) fusion(pred[2048]{0:T(1024)(128)(4,1)S(1)} %compare_reduce_fusion, pred[2048]{0:T(1024)(128)(4,1)S(1)} %compare_reduce_fusion.1, pred[2048]{0:T(1024)(128)(4,1)S(1)} %compare_reduce_fusion.2, pred[2048]{0:T(1024)(128)(4,1)S(1)} %compare_reduce_fusion.3, ...), kind=kLoop, calls=%fused_computation.112 | loop fusion | flops 69632 | bytes 69732 | tf_op jit(solution)/shard_map/ge | solution.py:89
  32.5 0.9 copy.61
  33.4 0.3 multiply_cosine_fusion
  33.7 0.2 fusion.38
  33.9 1.0 copy.62
  35.3 20.5 %all-gather = bf16[2048,1,128]{0,2,1:T(8,128)(2,1)S(1)} all-gather(bf16[128,1,128]{0,2,1:T(8,128)(2,1)S(1)} %pad_maximum_fusion.1), channel_id=2, replica_groups=mesh['seq'=16,'exp'=8] {'seq'}, dimensions={0}, use_global_device_ids=true | all-gather | bytes 557056 | tf_op jit(solution)/shard_map/all_gather | solution.py:75
  55.8 18.2 %all_gather.10 = bf16[2048,128]{1,0:T(8,128)(2,1)S(1)} all-gather(bf16[128,128]{1,0:T(8,128)(2,1)} %param.16), channel_id=1, replica_groups=mesh['seq'=16,'exp'=8] {'seq'}, dimensions={0}, use_global_device_ids=true | all-gather | bytes 557056 | tf_op jit(solution)/shard_map/all_gather | solution.py:76
  74.0 1.5 compare_and_fusion
  75.6 0.8 fusion.7
  76.5 1.0 fusion.8
  77.5 1.1 fusion.22
  78.6 1.1 copy-done
  79.7 1.7 convolution_convert_fusion
  82.3 39.0 %reduce-scatter.3.cloned.1.call-done = bf16[128,512]{1,0:T(8,128)(2,1)} async-done(((bf16[128,4096]{1,0:T(8,128)(2,1)}), bf16[128,512]{1,0:T(8,128)(2,1)}) %reduce-scatter.3.cloned.1.call-update) | async-done | bytes 131088 | tf_op jit(solution)/shard_map/reduce_scatter | solution.py:113
  121.3 1.2 convolution_convert_fusion.1
  122.5 15.3 %all_to_all.8 = bf16[8,64,512]{2,1,0:T(8,128)(2,1)S(1)} all-to-all(bf16[8,64,512]{2,1,0:T(8,128)(2,1)S(1)} %bitcast.130), channel_id=1, replica_groups=mesh['seq'=16,'exp'=8] {'exp'}, dimensions={0} | all-to-all | bytes 1048576 | tf_op jit(solution)/shard_map/all_to_all | solution.py:138
  137.8 0.2 fusion.25
  138.3 1.0 multiply_convert_fusion.1
  139.3 0.2 reduce-scatter.5.cloned.1.call-start
  139.5 70.0 %all-gather.3.cloned.1.call-done = bf16[1,1024,4096]{2,1,0:T(8,128)(2,1)} async-done(((bf16[1,64,4096]{2,1,0:T(8,128)(2,1)}), bf16[1,1024,4096]{2,1,0:T(8,128)(2,1)}) %all-gather.3.cloned.1.call-update) | async-done | bytes 8388624 | tf_op jit(solution)/shard_map/all_gather | solution.py:148
  209.5 12.5 %fusion = f32[1024,896]{1,0:T(8,128)S(1)} fusion(bf16[1,1024,4096]{2,1,0:T(8,128)(2,1)} %all-gather.3.cloned.1.call-done, bf16[1,4096,896]{2,1,0:T(8,128)(2,1)} %param.24), kind=kOutput, calls=%fused_computation.4 | convolution fusion | flops 7516192768 | bytes 19398656 | tf_op jit(solution)/shard_map/end,edf->enf/dot_general | solution.py:150
  222.0 12.1 %multiply_convert_fusion = bf16[1024,896]{1,0:T(8,128)(2,1)S(1)} fusion(f32[1024,896]{1,0:T(8,128)S(1)} %fusion, bf16[1,4096,896]{2,1,0:T(8,128)(2,1)} %param.23, bf16[1,1024,4096]{2,1,0:T(8,128)(2,1)S(1)} %copy-done.6), kind=kOutput, calls=%fused_computation.16 | convolution fusion | flops 7521697792 | bytes 21233664 | tf_op jit(solution)/shard_map/end,edf->enf/dot_general | solution.py:149
  234.1 11.1 %convert_bitcast_fusion = bf16[1024,1,4096]{2,0,1:T(8,128)(2,1)} fusion(bf16[1024,896]{1,0:T(8,128)(2,1)S(1)} %multiply_convert_fusion, bf16[1,896,4096]{2,1,0:T(8,128)(2,1)S(1)} %bitcast.138), kind=kOutput, calls=%fused_computation.8 | convolution fusion | flops 7520387072 | bytes 17563648 | tf_op jit(solution)/shard_map/enf,efd->ned/dot_general | solution.py:153
  245.2 0.6 copy-done.7
  245.9 2.5 sort.35
  248.6 5.0 %sort.34 = (s32[2048]{0:T(1024)}, s32[2048]{0:T(1024)S(1)}) sort(s32[2048]{0:T(1024)S(1)} %get-tuple-element.7, s32[2048]{0:T(1024)S(1)} %iota.49), dimensions={0}, to_apply=%region_9.10 | sort | flops 22528 | bytes 32768 | tf_op jit(solution)/shard_map/jit(argsort)/sort | solution.py:68
  253.7 1.1 gather_fusion.1
  254.9 74.9 %reduce-scatter.5.cloned.1.call-done = bf16[64,1,4096]{2,0,1:T(8,128)(2,1)} async-done(((bf16[1024,1,4096]{2,0,1:T(8,128)(2,1)}), bf16[64,1,4096]{2,0,1:T(8,128)(2,1)}) %reduce-scatter.5.cloned.1.call-update) | async-done | bytes 524304 | tf_op jit(solution)/shard_map/reduce_scatter | solution.py:152
  329.8 4.9 %copy.70 = bf16[64,1,4096]{0,1,2:T(2,128)(2,1)S(1)} copy(bf16[64,1,4096]{2,0,1:T(8,128)(2,1)} %reduce-scatter.5.cloned.1.call-done) | data formatting | bytes 1048576 | tf_op jit(solution)/shard_map/reduce_scatter | solution.py:152
  334.7 0.5 broadcast.624
  335.2 23.6 %reduce.56 = bf16[4096,64]{1,0:T(8,128)(2,1)} reduce(bf16[4096,1,64]{2,1,0:T(2,128)(2,1)S(1)} %bitcast.127, bf16[]{:T(256)} %broadcast.624), dimensions={1}, to_apply=%bitcast.118.reduce_sub_computation | reduce | bytes 1048578
  358.8 3.0 reshape.625
  361.8 6.6 %all-to-all-start.1 = ((bf16[8,2,16384]{2,1,0:T(2,128)(2,1)}), bf16[8,2,16384]{2,1,0:T(2,128)(2,1)S(1)}, u32[]{:S(2)}, u32[]{:S(2)}) async-start(bf16[8,2,16384]{2,1,0:T(2,128)(2,1)} %reshape.625), calls=%async_computation.3 | async-start | bytes 1048576 | tf_op jit(solution)/shard_map/all_to_all | solution.py:160
  368.6 0.7 gather_fusion.3
  369.4 0.3 copy.73
  369.7 0.7 gather_fusion.2
  370.5 0.8 pad_maximum_fusion
  371.3 6.5 %all-to-all-done.1 = bf16[8,2,16384]{2,1,0:T(2,128)(2,1)S(1)} async-done(((bf16[8,2,16384]{2,1,0:T(2,128)(2,1)}), bf16[8,2,16384]{2,1,0:T(2,128)(2,1)S(1)}, u32[]{:S(2)}, u32[]{:S(2)}) %all-to-all-start.1) | async-done | bytes 524320 | tf_op jit(solution)/shard_map/all_to_all | solution.py:160
  377.7 1.2 reshape.626
  379.0 2.3 copy.71
  381.2 0.2 reshape.440
  381.5 1.2 gather_fusion
  382.6 0.3 reshape.447
  383.0 0.7 multiply_reduce_fusion
  383.7 0.7 add_convert_fusion
  (88 shorter events, 3.4 us)
Async XLA Ops:
  7.2 114.1 %reduce-scatter.3.cloned.1.call-start = ((), (), s32[]{:S(2)}) async-start(), calls=%async_computation.4 | async-start | bytes 1179648 | tf_op jit(solution)/shard_map/reduce_scatter | solution.py:113
  77.5 2.2 copy-start
  78.6 2.9 copy-start.4
  78.6 42.7 %copy-start.1 = (bf16[128,512]{1,0:T(8,128)(2,1)S(1)}, bf16[128,512]{1,0:T(8,128)(2,1)}, u32[]{:S(2)}) copy-start(bf16[128,512]{1,0:T(8,128)(2,1)} %param.13) | copy-start | bytes 393220
  81.4 56.8 %copy-start.3 = (f32[4096]{0:T(1024)S(1)}, f32[4096]{0:T(1024)}, u32[]{:S(2)}) copy-start(f32[4096]{0:T(1024)} %param.20) | copy-start | bytes 49156
  81.4 128.1 %all-gather.3.cloned.1.call-start = ((), (), s32[]{:S(2)}) async-start(), calls=%async_computation.5 | async-start | bytes 8912896 | tf_op jit(solution)/shard_map/all_gather | solution.py:148
  139.3 190.5 %reduce-scatter.5.cloned.1.call-start = ((), (), s32[]{:S(2)}) async-start(), calls=%async_computation.6 | async-start | bytes 8912896 | tf_op jit(solution)/shard_map/reduce_scatter | solution.py:152
  209.5 12.5 %copy-start.6 = (bf16[1,1024,4096]{2,1,0:T(8,128)(2,1)S(1)}, bf16[1,1024,4096]{2,1,0:T(8,128)(2,1)}, u32[]{:S(2)}) copy-start(bf16[1,1024,4096]{2,1,0:T(8,128)(2,1)} %all-gather.3.cloned.1.call-done) | copy-start | bytes 25165828
  209.5 24.6 %slice-start = ((s8[7340032]{0:T(1024)(128)(4,1)}), s8[4194304]{0:T(1024)(128)(4,1)S(1)}, s32[]{:S(2)}) async-start(s8[7340032]{0:T(1024)(128)(4,1)} %bitcast.137), calls=%async_computation.7 | async-start | bytes 8388608
  222.0 12.1 %slice-start.1 = ((s8[7340032]{0:T(1024)(128)(4,1)}), s8[3145728]{0:T(1024)(128)(4,1)S(1)}, s32[]{:S(2)}) async-start(s8[7340032]{0:T(1024)(128)(4,1)} %bitcast.137), calls=%async_computation.8 | async-start | bytes 6291456
  245.2 0.7 copy-start.7
  245.2 8.5 %copy-start.5 = (f32[128,2]{0,1:T(2,128)S(1)}, f32[128,2]{0,1:T(2,128)}, u32[]{:S(2)}) copy-start(f32[128,2]{0,1:T(2,128)} %param.21) | copy-start | bytes 3076
  361.8 15.9 %all-to-all-start.1 = ((bf16[8,2,16384]{2,1,0:T(2,128)(2,1)}), bf16[8,2,16384]{2,1,0:T(2,128)(2,1)S(1)}, u32[]{:S(2)}, u32[]{:S(2)}) async-start(bf16[8,2,16384]{2,1,0:T(2,128)(2,1)} %reshape.625), calls=%async_computation.3 | async-start | bytes 1048576 | tf_op jit(solution)/shard_map/all_to_all | solution.py:160
  379.0 4.7 %copy-start.2 = (bf16[128,512]{1,0:T(8,128)(2,1)S(1)}, bf16[128,512]{1,0:T(8,128)(2,1)}, u32[]{:S(2)}) copy-start(bf16[128,512]{1,0:T(8,128)(2,1)} %reduce-scatter.3.cloned.1.call-done) | copy-start | bytes 393220
Sparse Core Ops, SparseCore 0:
  81.6 39.6 reduce-scatter.2
  139.4 70.0 all-gather.2
  245.4 84.3 reduce-scatter.4
where the time goes:
time: 392 us; the launch traced here: 391 us
  waiting for transfers between devices  190 us (48%)
  other arithmetic  59.5 us (15%)
  blocking collectives  54.1 us (14%)
  matrix products  40.6 us (10%)
  local copies, waits for them, and re-layouts  25.3 us (6%)
  between operations  14.2 us (4%)
  starting transfers between devices  6.86 us (2%)
    reduce_scatter x1, waiting for transfers between devices, per_device(): lax.psum_scatter(jnp.einsum('enf,efd->ned', hidden_units, w_down, preferr...  74.9 us
    all_gather x1, waiting for transfers between devices, per_device(): token_rows = lax.all_gather(normed, 'seq', axis=1, tiled=True)  70 us
    reduce_scatter x1, waiting for transfers between devices, per_device(): lax.psum_scatter(partial_proj.astype(jnp.bfloat16), 'exp', scatter_dimens...  39 us
    unnamed x3, other arithmetic  23.7 us
    all_gather x1, blocking collectives, per_device(): lax.all_gather(key_rotated, 'seq', axis=0, tiled=True)  20.5 us
    all_gather x1, blocking collectives, per_device(): lax.all_gather(values, 'seq', axis=0, tiled=True)  18.2 us
    ge x1, other arithmetic, per_device(): all_pos >= long_len  15.8 us
    all_to_all x1, blocking collectives, per_device(): lax.all_to_all(outgoing_rows.reshape(exp_count, expert_local * capacity,...  15.3 us
  transfers between devices with their start and end apart: 4, of which 4 were waited for; matrix products, arithmetic and copies ran while one was open for 3% of the time, Pallas kernels for 0%

commit v1 on v0

--- a/solution.py
+++ b/solution.py
@@ -157,7 +157,18 @@
         scatter_dimension=0,
         tiled=True,
     )
-    homed = lax.all_to_all(returned, "exp", split_axis=2, concat_axis=1, tiled=True)
+    ways, here = (lax.axis_size("exp"), lax.axis_index("exp"))
+    width = returned.shape[2] // ways
+    lengths = list(returned.shape)
+    lengths[2] = width
+    height = lengths[1]
+    lengths[1] = height * ways
+    homed = jnp.zeros(lengths, returned.dtype)
+    for mask in range(ways):
+        part = lax.dynamic_slice_in_dim(returned, (here ^ mask) * width, width, axis=2)
+        if mask:
+            part = lax.ppermute(part, "exp", [(d, d ^ mask) for d in range(ways)])
+        homed = lax.dynamic_update_slice_in_dim(homed, part, (here ^ mask) * height, axis=1)
     lookup = homed.reshape(capacity * NEXP, -1)
     chosen = (
         lookup[(slot_rank * NEXP + routes).reshape(assign_count)]

time: 392 us -> 361 us (0.921)
  other arithmetic: 59.5 us -> 35.9 us
  local copies, waits for them, and re-layouts: 25.3 us -> 15.8 us
    unnamed x3 -> x2, other arithmetic: 23.7 us -> 0.13 us
    ppermute x0 -> x7, waiting for transfers between devices: none -> 9.4 us  [per_device(): part = lax.ppermute(part, 'exp', [(d, d ^ mask) for d in range(ways)])]
    ppermute x0 -> x7, starting transfers between devices: none -> 8.9 us  [per_device(): part = lax.ppermute(part, 'exp', [(d, d ^ mask) for d in range(ways)])]
    all_to_all x1 -> x0, starting transfers between devices: 6.55 us -> none  [per_device(): lax.all_to_all(returned, 'exp', split_axis=2, concat_axis=1, tiled=True)]
    all_to_all x1 -> x0, waiting for transfers between devices: 6.46 us -> none  [per_device(): lax.all_to_all(returned, 'exp', split_axis=2, concat_axis=1, tiled=True)]
    reduce_scatter x1 -> x0, local copies, waits for them, and re-layouts: 4.86 us -> none  [per_device(): lax.psum_scatter(jnp.einsum('enf,efd->ned', hidden_units, w_down, preferr...]
    unnamed x28 -> x25, local copies, waits for them, and re-layouts: 8.75 us -> 3.91 us
  transfers between devices with their start and end apart: 4 -> 10, of which waited for: 4 -> 5; matrix products, arithmetic and copies ran while one was open for 3% -> 4% of each run, Pallas kernels for 0% -> 0%
where the time goes in v1:
time: 361 us; the launch traced here: 360 us
  waiting for transfers between devices  190 us (53%)
  blocking collectives  54.1 us (15%)
  matrix products  40.7 us (11%)
  other arithmetic  35.9 us (10%)
  local copies, waits for them, and re-layouts  15.8 us (4%)
  between operations  14.4 us (4%)
  starting transfers between devices  9.2 us (3%)
    reduce_scatter x1, waiting for transfers between devices, per_device(): lax.psum_scatter(jnp.einsum('enf,efd->ned', hidden_units, w_down, preferr...  71.8 us
    all_gather x1, waiting for transfers between devices, per_device(): token_rows = lax.all_gather(normed, 'seq', axis=1, tiled=True)  70 us
    reduce_scatter x1, waiting for transfers between devices, per_device(): lax.psum_scatter(partial_proj.astype(jnp.bfloat16), 'exp', scatter_dimens...  39 us
    all_gather x1, blocking collectives, per_device(): lax.all_gather(key_rotated, 'seq', axis=0, tiled=True)  20.5 us
    all_gather x1, blocking collectives, per_device(): lax.all_gather(values, 'seq', axis=0, tiled=True)  18.2 us
    ge x1, other arithmetic, per_device(): all_pos >= long_len  15.8 us
    all_to_all x1, blocking collectives, per_device(): lax.all_to_all(outgoing_rows.reshape(exp_count, expert_local * capacity,...  15.3 us
    dot_general x1, matrix products, per_device(): jnp.einsum('end,edf->enf', token_rows, w_up, preferred_element_type=jnp.f...  12.5 us
  transfers between devices with their start and end apart: 10, of which 5 were waited for; matrix products, arithmetic and copies ran while one was open for 4% of the time, Pallas kernels for 0%

profile of v1, /device:TPU:1, one launch (start us, length us, event | category | flops | bytes accessed | tf_op | source)
XLA Modules:
  0.0 360.3 jit_solution(15924470454836005255)
XLA Ops:
  8.4 1.8 fusion.55
  10.2 2.1 fusion.54
  12.3 4.3 %compare_select_fusion.1 = s32[2048,1]{0,1:T(1,128)S(1)} fusion(s32[]{:T(128)} %bitcast.25, s32[]{:T(128)} %bitcast.26, s32[]{:T(128)} %bitcast.27, s32[]{:T(128)} %bitcast.28, s32[]{:T(128)} %bitcast.29, s32[]{:T(128)} %bitcast.31, s32[]{:T(128)} %bitcast.30), kind=kLoop, calls=%fused_computation.89 | loop fusion | flops 47104 | bytes 8220 | tf_op jit(solution)/shard_map/gather | solution.py:54
  16.7 15.8 %broadcast_compare_fusion = (pred[2048]{0:T(1024)(128)(4,1)S(1)}, s32[2048]{0:T(1024)S(1)}) fusion(pred[2048]{0:T(1024)(128)(4,1)S(1)} %compare_reduce_fusion, pred[2048]{0:T(1024)(128)(4,1)S(1)} %compare_reduce_fusion.1, pred[2048]{0:T(1024)(128)(4,1)S(1)} %compare_reduce_fusion.2, pred[2048]{0:T(1024)(128)(4,1)S(1)} %compare_reduce_fusion.3, ...), kind=kLoop, calls=%fused_computation.113 | loop fusion | flops 69632 | bytes 69732 | tf_op jit(solution)/shard_map/ge | solution.py:89
  32.5 0.9 copy.65
  33.4 0.3 multiply_cosine_fusion
  33.9 1.0 copy.66
  35.3 20.5 %all-gather = bf16[2048,1,128]{0,2,1:T(8,128)(2,1)S(1)} all-gather(bf16[128,1,128]{0,2,1:T(8,128)(2,1)S(1)} %pad_maximum_fusion.1), channel_id=2, replica_groups=mesh['seq'=16,'exp'=8] {'seq'}, dimensions={0}, use_global_device_ids=true | all-gather | bytes 557056 | tf_op jit(solution)/shard_map/all_gather | solution.py:75
  55.8 18.2 %all_gather.10 = bf16[2048,128]{1,0:T(8,128)(2,1)S(1)} all-gather(bf16[128,128]{1,0:T(8,128)(2,1)} %param.16), channel_id=1, replica_groups=mesh['seq'=16,'exp'=8] {'seq'}, dimensions={0}, use_global_device_ids=true | all-gather | bytes 557056 | tf_op jit(solution)/shard_map/all_gather | solution.py:76
  74.1 1.5 compare_and_fusion
  75.6 0.8 fusion.7
  76.5 1.0 fusion.8
  77.5 1.1 fusion.22
  78.6 1.1 copy-done
  79.7 1.7 convolution_convert_fusion
  82.3 39.0 %reduce-scatter.3.cloned.1.call-done = bf16[128,512]{1,0:T(8,128)(2,1)} async-done(((bf16[128,4096]{1,0:T(8,128)(2,1)}), bf16[128,512]{1,0:T(8,128)(2,1)}) %reduce-scatter.3.cloned.1.call-update) | async-done | bytes 131088 | tf_op jit(solution)/shard_map/reduce_scatter | solution.py:113
  121.3 1.2 convolution_convert_fusion.1
  122.5 15.3 %all_to_all.4 = bf16[8,64,512]{2,1,0:T(8,128)(2,1)S(1)} all-to-all(bf16[8,64,512]{2,1,0:T(8,128)(2,1)S(1)} %bitcast.126), channel_id=1, replica_groups=mesh['seq'=16,'exp'=8] {'exp'}, dimensions={0} | all-to-all | bytes 1048576 | tf_op jit(solution)/shard_map/all_to_all | solution.py:138
  137.8 0.2 fusion.25
  138.3 1.0 multiply_convert_fusion.1
  139.3 0.2 reduce-scatter.5.cloned.1.call-start
  139.5 70.0 %all-gather.3.cloned.1.call-done = bf16[1,1024,4096]{2,1,0:T(8,128)(2,1)} async-done(((bf16[1,64,4096]{2,1,0:T(8,128)(2,1)}), bf16[1,1024,4096]{2,1,0:T(8,128)(2,1)}) %all-gather.3.cloned.1.call-update) | async-done | bytes 8388624 | tf_op jit(solution)/shard_map/all_gather | solution.py:148
  209.5 12.5 %fusion = f32[1024,896]{1,0:T(8,128)S(1)} fusion(bf16[1,1024,4096]{2,1,0:T(8,128)(2,1)} %all-gather.3.cloned.1.call-done, bf16[1,4096,896]{2,1,0:T(8,128)(2,1)} %param.24), kind=kOutput, calls=%fused_computation.4 | convolution fusion | flops 7516192768 | bytes 19398656 | tf_op jit(solution)/shard_map/end,edf->enf/dot_general | solution.py:150
  222.0 12.1 %multiply_convert_fusion = bf16[1024,896]{1,0:T(8,128)(2,1)S(1)} fusion(f32[1024,896]{1,0:T(8,128)S(1)} %fusion, bf16[1,4096,896]{2,1,0:T(8,128)(2,1)} %param.23, bf16[1,1024,4096]{2,1,0:T(8,128)(2,1)S(1)} %copy-done.6), kind=kOutput, calls=%fused_computation.16 | convolution fusion | flops 7521697792 | bytes 21233664 | tf_op jit(solution)/shard_map/end,edf->enf/dot_general | solution.py:149
  234.1 11.1 %convert_bitcast_fusion = bf16[1024,1,4096]{2,0,1:T(8,128)(2,1)} fusion(bf16[1024,896]{1,0:T(8,128)(2,1)S(1)} %multiply_convert_fusion, bf16[1,896,4096]{2,1,0:T(8,128)(2,1)S(1)} %bitcast.134), kind=kOutput, calls=%fused_computation.8 | convolution fusion | flops 7520387072 | bytes 17563648 | tf_op jit(solution)/shard_map/enf,efd->ned/dot_general | solution.py:153
  245.3 0.5 copy-done.7
  245.9 2.5 sort.35
  248.6 5.0 %sort.34 = (s32[2048]{0:T(1024)}, s32[2048]{0:T(1024)S(1)}) sort(s32[2048]{0:T(1024)S(1)} %get-tuple-element.7, s32[2048]{0:T(1024)S(1)} %iota.49), dimensions={0}, to_apply=%region_9.10 | sort | flops 22528 | bytes 32768 | tf_op jit(solution)/shard_map/jit(argsort)/sort | solution.py:68
  254.0 1.1 gather_fusion.1
  255.2 0.7 gather_fusion.3
  256.0 0.3 copy.77
  256.2 0.7 gather_fusion.2
  257.1 0.8 pad_maximum_fusion
  257.9 71.8 %reduce-scatter.5.cloned.1.call-done = bf16[64,1,4096]{2,0,1:T(8,128)(2,1)} async-done(((bf16[1024,1,4096]{2,0,1:T(8,128)(2,1)}), bf16[64,1,4096]{2,0,1:T(8,128)(2,1)}) %reduce-scatter.5.cloned.1.call-update) | async-done | bytes 524304 | tf_op jit(solution)/shard_map/reduce_scatter | solution.py:152
  329.7 1.1 constant_dynamic-slice_fusion
  330.9 2.2 collective-permute-start
  333.1 2.7 collective-permute-start.6
  335.9 2.1 collective-permute-start.4
  338.0 1.3 collective-permute-start.3
  339.3 0.3 collective-permute-start.1
  339.6 5.4 %collective-permute-done.1 = bf16[64,1,512]{2,0,1:T(8,128)(2,1)S(1)} collective-permute-done((bf16[64,1,512]{2,0,1:T(8,128)(2,1)S(1)}, bf16[64,1,512]{2,0,1:T(8,128)(2,1)S(1)}, u32[]{:S(2)}, u32[]{:S(2)}) %collective-permute-start.1) | collective-permute-done | bytes 65568 | tf_op jit(solution)/shard_map/ppermute | solution.py:170
  345.2 4.0 %collective-permute-done.2 = bf16[64,1,512]{2,0,1:T(8,128)(2,1)S(1)} collective-permute-done((bf16[64,1,512]{2,0,1:T(8,128)(2,1)S(1)}, bf16[64,1,512]{2,0,1:T(8,128)(2,1)S(1)}, u32[]{:S(2)}, u32[]{:S(2)}) %collective-permute-start.2) | collective-permute-done | bytes 65568 | tf_op jit(solution)/shard_map/ppermute | solution.py:170
  349.3 0.3 copy.74
  349.7 1.2 dynamic_update_slice.31
  350.9 1.2 gather_fusion
  352.0 0.3 reshape.443
  352.4 0.7 multiply_reduce_fusion
  353.1 0.7 add_convert_fusion
  (104 shorter events, 4.1 us)
Async XLA Ops:
  7.2 114.1 %reduce-scatter.3.cloned.1.call-start = ((), (), s32[]{:S(2)}) async-start(), calls=%async_computation.3 | async-start | bytes 1179648 | tf_op jit(solution)/shard_map/reduce_scatter | solution.py:113
  77.5 2.2 copy-start
  78.6 2.9 copy-start.4
  78.6 42.7 %copy-start.1 = (bf16[128,512]{1,0:T(8,128)(2,1)S(1)}, bf16[128,512]{1,0:T(8,128)(2,1)}, u32[]{:S(2)}) copy-start(bf16[128,512]{1,0:T(8,128)(2,1)} %param.13) | copy-start | bytes 393220
  81.4 56.8 %copy-start.3 = (f32[4096]{0:T(1024)S(1)}, f32[4096]{0:T(1024)}, u32[]{:S(2)}) copy-start(f32[4096]{0:T(1024)} %param.20) | copy-start | bytes 49156
  81.5 128.1 %all-gather.3.cloned.1.call-start = ((), (), s32[]{:S(2)}) async-start(), calls=%async_computation.4 | async-start | bytes 8912896 | tf_op jit(solution)/shard_map/all_gather | solution.py:148
  139.3 190.4 %reduce-scatter.5.cloned.1.call-start = ((), (), s32[]{:S(2)}) async-start(), calls=%async_computation.5 | async-start | bytes 8912896 | tf_op jit(solution)/shard_map/reduce_scatter | solution.py:152
  209.5 12.5 %copy-start.6 = (bf16[1,1024,4096]{2,1,0:T(8,128)(2,1)S(1)}, bf16[1,1024,4096]{2,1,0:T(8,128)(2,1)}, u32[]{:S(2)}) copy-start(bf16[1,1024,4096]{2,1,0:T(8,128)(2,1)} %all-gather.3.cloned.1.call-done) | copy-start | bytes 25165828
  209.5 24.6 %slice-start = ((s8[7340032]{0:T(1024)(128)(4,1)}), s8[4194304]{0:T(1024)(128)(4,1)S(1)}, s32[]{:S(2)}) async-start(s8[7340032]{0:T(1024)(128)(4,1)} %bitcast.133), calls=%async_computation.6 | async-start | bytes 8388608
  222.0 12.1 %slice-start.1 = ((s8[7340032]{0:T(1024)(128)(4,1)}), s8[3145728]{0:T(1024)(128)(4,1)S(1)}, s32[]{:S(2)}) async-start(s8[7340032]{0:T(1024)(128)(4,1)} %bitcast.133), calls=%async_computation.7 | async-start | bytes 6291456
  245.2 0.7 copy-start.7
  245.2 8.5 %copy-start.5 = (f32[128,2]{0,1:T(2,128)S(1)}, f32[128,2]{0,1:T(2,128)}, u32[]{:S(2)}) copy-start(f32[128,2]{0,1:T(2,128)} %param.21) | copy-start | bytes 3076
  256.2 96.8 %copy-start.2 = (bf16[128,512]{1,0:T(8,128)(2,1)S(1)}, bf16[128,512]{1,0:T(8,128)(2,1)}, u32[]{:S(2)}) copy-start(bf16[128,512]{1,0:T(8,128)(2,1)} %reduce-scatter.3.cloned.1.call-done) | copy-start | bytes 393220
  330.9 8.5 %collective-permute-start = (bf16[64,1,512]{2,0,1:T(8,128)(2,1)S(1)}, bf16[64,1,512]{2,0,1:T(8,128)(2,1)S(1)}, u32[]{:S(2)}, u32[]{:S(2)}) collective-permute-start(bf16[64,1,512]{2,0,1:T(8,128)(2,1)S(1)} %get-tuple-element.18), channel_id=1, source_target_pairs={{0,1},{1,0},{2,3},{3,2},{4,5},{5,4},{6,7},{7,6},{8,9},{9,8},{10,11... | collective-permute-start | bytes 196616 | tf_op jit(solution)/shard_map/ppermute | solution.py:170
  333.1 16.5 %collective-permute-start.6 = (bf16[64,1,512]{2,0,1:T(8,128)(2,1)S(1)}, bf16[64,1,512]{2,0,1:T(8,128)(2,1)S(1)}, u32[]{:S(2)}, u32[]{:S(2)}) collective-permute-start(bf16[64,1,512]{2,0,1:T(8,128)(2,1)S(1)} %get-tuple-element.12), channel_id=1, source_target_pairs={{0,7},{1,6},{2,5},{3,4},{4,3},{5,2},{6,1},{7,0},{8,15},{9,14},{10,... | collective-permute-start | bytes 196616 | tf_op jit(solution)/shard_map/ppermute | solution.py:170
  335.8 13.5 %collective-permute-start.5 = (bf16[64,1,512]{2,0,1:T(8,128)(2,1)S(1)}, bf16[64,1,512]{2,0,1:T(8,128)(2,1)S(1)}, u32[]{:S(2)}, u32[]{:S(2)}) collective-permute-start(bf16[64,1,512]{2,0,1:T(8,128)(2,1)S(1)} %get-tuple-element.13), channel_id=1, source_target_pairs={{0,6},{1,7},{2,4},{3,5},{4,2},{5,3},{6,0},{7,1},{8,14},{9,15},{10,... | collective-permute-start | bytes 196616 | tf_op jit(solution)/shard_map/ppermute | solution.py:170
  335.9 13.3 %collective-permute-start.4 = (bf16[64,1,512]{2,0,1:T(8,128)(2,1)S(1)}, bf16[64,1,512]{2,0,1:T(8,128)(2,1)S(1)}, u32[]{:S(2)}, u32[]{:S(2)}) collective-permute-start(bf16[64,1,512]{2,0,1:T(8,128)(2,1)S(1)} %get-tuple-element.14), channel_id=1, source_target_pairs={{0,5},{1,4},{2,7},{3,6},{4,1},{5,0},{6,3},{7,2},{8,13},{9,12},{10,... | collective-permute-start | bytes 196616 | tf_op jit(solution)/shard_map/ppermute | solution.py:170
  338.0 11.2 %collective-permute-start.3 = (bf16[64,1,512]{2,0,1:T(8,128)(2,1)S(1)}, bf16[64,1,512]{2,0,1:T(8,128)(2,1)S(1)}, u32[]{:S(2)}, u32[]{:S(2)}) collective-permute-start(bf16[64,1,512]{2,0,1:T(8,128)(2,1)S(1)} %get-tuple-element.15), channel_id=1, source_target_pairs={{0,4},{1,5},{2,6},{3,7},{4,0},{5,1},{6,2},{7,3},{8,12},{9,13},{10,... | collective-permute-start | bytes 196616 | tf_op jit(solution)/shard_map/ppermute | solution.py:170
  339.3 5.8 %collective-permute-start.1 = (bf16[64,1,512]{2,0,1:T(8,128)(2,1)S(1)}, bf16[64,1,512]{2,0,1:T(8,128)(2,1)S(1)}, u32[]{:S(2)}, u32[]{:S(2)}) collective-permute-start(bf16[64,1,512]{2,0,1:T(8,128)(2,1)S(1)} %get-tuple-element.17), channel_id=1, source_target_pairs={{0,2},{1,3},{2,0},{3,1},{4,6},{5,7},{6,4},{7,5},{8,10},{9,11},{10,... | collective-permute-start | bytes 196616 | tf_op jit(solution)/shard_map/ppermute | solution.py:170
  345.1 4.1 %collective-permute-start.2 = (bf16[64,1,512]{2,0,1:T(8,128)(2,1)S(1)}, bf16[64,1,512]{2,0,1:T(8,128)(2,1)S(1)}, u32[]{:S(2)}, u32[]{:S(2)}) collective-permute-start(bf16[64,1,512]{2,0,1:T(8,128)(2,1)S(1)} %get-tuple-element.16), channel_id=1, source_target_pairs={{0,3},{1,2},{2,1},{3,0},{4,7},{5,6},{6,5},{7,4},{8,11},{9,10},{10,... | collective-permute-start | bytes 196616 | tf_op jit(solution)/shard_map/ppermute | solution.py:170
Sparse Core Ops, SparseCore 0:
  81.6 39.6 reduce-scatter.2
  139.4 70.0 all-gather.2
  245.4 84.2 reduce-scatter.4
